TPU v7x, 256 devices: a whole 4x4x8 slice. The times are simulated.
256 devices in a mesh: expert: 64 (over x, z, core), tensor: 4 (over y).
Axes of the slice: x: 4, y: 4, z: 8, core: 2. Of those that a mesh axis runs over, the one named last changes fastest.
Arguments:
- tokens: bfloat16 [8192, 3584], P('expert'), may hold values from -6 to 6
- cotangent: bfloat16 [8192, 3584], P('expert'), may hold values from -6 to 6
- chosen_experts: int32 [8192, 8], P('expert'), may hold values from 0 to 255, as said below
- chosen_slots: int32 [8192, 8], P('expert'), may hold values from 0 to 127, as said below
- routing_gate_weight: float32 [8192, 8], P('expert'), may hold values from 0.1 to 1
- padded_slot_count: int32 [64, 64], P('expert'), may hold values from 0 to 8, as said below
- w_gate: bfloat16 [64, 3584, 1024], P('expert', None, 'tensor'), may hold values from -0.09375 to 0.09375
- w_up: bfloat16 [64, 3584, 1024], P('expert', None, 'tensor'), may hold values from -0.09375 to 0.09375
- w_down: bfloat16 [64, 1024, 3584], P('expert', 'tensor'), may hold values from -0.1875 to 0.1875
Outputs:
- mixed: bfloat16 [8192, 3584], P('expert', 'tensor')
- token_gradient: bfloat16 [8192, 3584], P('expert', 'tensor')
- gate_gradient: float32 [8192, 8], P('expert')
- grad_w_gate: bfloat16 [64, 3584, 1024], P('expert', None, 'tensor')
- grad_w_up: bfloat16 [64, 3584, 1024], P('expert', None, 'tensor')
- grad_w_down: bfloat16 [64, 1024, 3584], P('expert', 'tensor')
Inputs may be any that keep to these rules, and one draw needn't show every extreme that they name: `chosen_experts`: each token names 8 different experts; only experts under 64 are in flight. `chosen_slots`: within one block of 128 tokens, the routes that name one expert are numbered 0, 1, 2 and so on in order of token and then of route. In every block some expert in flight is named by every token. padded_slot_count[s, e] is the smaller of 8 and the number of routes of block s that name expert e; in every block some expert reaches 8, and some expert in flight is named by no route.
All inputs are finite; a program needn't handle non-finite values.
Results may differ from a plain program's by a relative error of at most 0.015.
Values may be sent and summed in bfloat16 or wider, within the bound.
No kernel may reach another device: no remote copies, remote signals or barrier semaphores. Data moves between devices by JAX's collectives and lax.ppermute only.
A program may use at most 128 MiB of HBM per device.

v0:
```python
import jax
import jax.numpy as jnp
from jax import lax
from jax.sharding import PartitionSpec as P

OWNED = 4


def routing_layout(chosen_expert, chosen_slot, slot_count_row, expert_capacity):
    expert_number = slot_count_row.shape[0]
    one_hot = (
        chosen_expert[:, :, None] == jnp.arange(expert_number, dtype=jnp.int32)[None, None, :]
    ).astype(jnp.int32)
    slot_ceiling = jnp.sum(one_hot * slot_count_row[None, None, :], axis=2)
    slot_alive_mask = (chosen_expert < expert_number) & (chosen_slot < slot_ceiling)
    destination_slot = jnp.where(slot_alive_mask, chosen_expert * expert_capacity + chosen_slot, -1)
    return (slot_alive_mask, destination_slot)


def pack_slots(tok_block, cot_block, block_gates, destination_slot, send_rows):
    select = destination_slot[None, :, :] == jnp.arange(send_rows, dtype=jnp.int32)[:, None, None]
    picked = jnp.sum(select.astype(jnp.int32), axis=2).astype(jnp.bfloat16)
    slot_gate = jnp.sum(jnp.where(select, block_gates[None, :, :], 0.0), axis=(1, 2))
    token_sum = jnp.dot(picked, tok_block, preferred_element_type=jnp.float32).astype(jnp.bfloat16)
    cot_sum = jnp.dot(picked, cot_block, preferred_element_type=jnp.float32)
    return (token_sum, (slot_gate[:, None] * cot_sum).astype(jnp.bfloat16))


def expert_group(expert_rows, expert_cots, gate_weight, up_weight, down_weight):
    pre_gate = jnp.dot(expert_rows, gate_weight, preferred_element_type=jnp.float32)
    pre_up = jnp.dot(expert_rows, up_weight, preferred_element_type=jnp.float32)
    logistic = jax.nn.sigmoid(pre_gate)
    active = pre_gate * logistic
    hidden = (active * pre_up).astype(jnp.bfloat16)
    part_out = jnp.dot(hidden, down_weight, preferred_element_type=jnp.float32)
    grad_hidden = jnp.dot(expert_cots, down_weight.T, preferred_element_type=jnp.float32)
    grad_pre_gate = (grad_hidden * pre_up * logistic * (1.0 + pre_gate * (1.0 - logistic))).astype(
        jnp.bfloat16
    )
    grad_pre_up = (grad_hidden * active).astype(jnp.bfloat16)
    part_back = jnp.dot(grad_pre_gate, gate_weight.T, preferred_element_type=jnp.float32) + jnp.dot(
        grad_pre_up, up_weight.T, preferred_element_type=jnp.float32
    )
    grad_gate_w = jnp.dot(expert_rows.T, grad_pre_gate, preferred_element_type=jnp.float32).astype(
        jnp.bfloat16
    )
    grad_up_w = jnp.dot(expert_rows.T, grad_pre_up, preferred_element_type=jnp.float32).astype(
        jnp.bfloat16
    )
    grad_down_w = jnp.dot(hidden.T, expert_cots, preferred_element_type=jnp.float32).astype(
        jnp.bfloat16
    )
    return (part_out, part_back, (grad_gate_w, grad_up_w, grad_down_w))


def expert_group_t(expert_rows, expert_cots, gate_weight, up_weight, down_weight):
    pre_gate = jnp.dot(expert_rows, gate_weight, preferred_element_type=jnp.float32)
    pre_up = jnp.dot(expert_rows, up_weight, preferred_element_type=jnp.float32)
    logistic = jax.nn.sigmoid(pre_gate)
    active = pre_gate * logistic
    hidden = (active * pre_up).astype(jnp.bfloat16)
    pre_gate, pre_up, logistic, active, hidden = lax.optimization_barrier(
        (pre_gate, pre_up, logistic, active, hidden)
    )
    n_tensor = lax.axis_size("tensor")
    share = gate_weight.shape[0] // n_tensor
    down_parts = down_weight.reshape(down_weight.shape[0], n_tensor, share)
    out_t = jnp.einsum(
        "mh,hkd->kmd", hidden, down_parts, preferred_element_type=jnp.float32
    ).astype(jnp.bfloat16)
    grad_hidden = jnp.dot(expert_cots, down_weight.T, preferred_element_type=jnp.float32)
    grad_pre_gate = (grad_hidden * pre_up * logistic * (1.0 + pre_gate * (1.0 - logistic))).astype(
        jnp.bfloat16
    )
    grad_pre_up = (grad_hidden * active).astype(jnp.bfloat16)
    gate_parts = gate_weight.reshape(n_tensor, share, gate_weight.shape[1])
    up_parts = up_weight.reshape(n_tensor, share, up_weight.shape[1])
    back_t = (
        jnp.einsum("mh,kdh->kmd", grad_pre_gate, gate_parts, preferred_element_type=jnp.float32)
        + jnp.einsum("mh,kdh->kmd", grad_pre_up, up_parts, preferred_element_type=jnp.float32)
    ).astype(jnp.bfloat16)
    grad_gate_w = jnp.dot(expert_rows.T, grad_pre_gate, preferred_element_type=jnp.float32).astype(
        jnp.bfloat16
    )
    grad_up_w = jnp.dot(expert_rows.T, grad_pre_up, preferred_element_type=jnp.float32).astype(
        jnp.bfloat16
    )
    grad_down_w = jnp.dot(hidden.T, expert_cots, preferred_element_type=jnp.float32).astype(
        jnp.bfloat16
    )
    return (out_t, back_t, (grad_gate_w, grad_up_w, grad_down_w))


def local(
    tokens,
    cotangent,
    chosen_experts,
    chosen_slots,
    routing_gate_weight,
    padded_slot_count,
    w_gate,
    w_up,
    w_down,
):
    tok_rows, feature_width = tokens.shape
    per_token = chosen_experts.shape[1]
    expert_number = padded_slot_count.shape[1]
    expert_capacity = 2 * tok_rows * per_token // (OWNED * lax.axis_size("expert"))
    send_rows = expert_number * expert_capacity
    feature_share = feature_width // lax.axis_size("tensor")
    first_col = lax.axis_index("tensor") * feature_share
    slot_alive_mask, destination_slot = routing_layout(
        chosen_experts, chosen_slots, padded_slot_count[0], expert_capacity
    )
    local_tokens = lax.dynamic_slice_in_dim(tokens, first_col, feature_share, 1)
    local_cotangent_bf = lax.dynamic_slice_in_dim(cotangent, first_col, feature_share, 1)
    token_sum, _ = pack_slots(
        local_tokens, local_cotangent_bf[:, :0], routing_gate_weight, destination_slot, send_rows
    )
    _, cot_rows = pack_slots(
        tokens[:, :0], cotangent, routing_gate_weight, destination_slot, send_rows
    )
    rows_q = lax.all_to_all(
        token_sum.reshape(expert_number, expert_capacity, feature_share),
        "expert",
        split_axis=0,
        concat_axis=0,
        tiled=True,
    ).reshape(send_rows, feature_share)
    rows_q, cot_rows = lax.optimization_barrier((rows_q, cot_rows))
    rows_all = lax.all_gather(rows_q, "tensor", axis=1, tiled=True)
    cots_all = lax.all_to_all(
        cot_rows.reshape(expert_number, expert_capacity, feature_width),
        "expert",
        split_axis=0,
        concat_axis=0,
        tiled=True,
    ).reshape(send_rows, feature_width)
    out_t, back_t, grads = expert_group_t(rows_all, cots_all, w_gate[0], w_up[0], w_down[0])
    total_out = lax.psum_scatter(out_t, "tensor", scatter_dimension=0, tiled=True)
    sources = total_out.shape[1] // expert_capacity
    came_out = lax.all_to_all(
        total_out.reshape(sources, expert_capacity, feature_share),
        "expert",
        split_axis=0,
        concat_axis=0,
        tiled=True,
    ).reshape(send_rows, feature_share)
    total_back = lax.psum_scatter(back_t, "tensor", scatter_dimension=0, tiled=True)
    came_back = lax.all_to_all(
        total_back.reshape(sources, expert_capacity, feature_share),
        "expert",
        split_axis=0,
        concat_axis=0,
        tiled=True,
    ).reshape(send_rows, feature_share)
    positions = jnp.maximum(destination_slot, 0).reshape(-1)
    out_rows = (
        jnp.take(came_out, positions, axis=0)
        .reshape(tok_rows, per_token, feature_share)
        .astype(jnp.float32)
    )
    gate_scaling = jnp.where(slot_alive_mask, routing_gate_weight, 0.0)
    mixed = jnp.sum(gate_scaling[:, :, None] * out_rows, axis=1).astype(jnp.bfloat16)
    route_hits = (
        destination_slot[None, :, :] == jnp.arange(send_rows, dtype=jnp.int32)[:, None, None]
    )
    slot_of_token = jnp.sum(route_hits.astype(jnp.int32), axis=2).astype(jnp.bfloat16)
    token_gradient = lax.dot_general(
        slot_of_token, came_back, (((0,), (0,)), ((), ())), preferred_element_type=jnp.float32
    ).astype(jnp.bfloat16)
    local_cotangent = local_cotangent_bf.astype(jnp.float32)
    hidden_totals = jnp.sum(local_cotangent[:, None, :] * out_rows, axis=2)
    gate_gradient = lax.psum(jnp.where(slot_alive_mask, hidden_totals, 0.0), "tensor")
    grad_gate_w, grad_up_w, grad_down_w = grads
    return (
        mixed,
        token_gradient,
        gate_gradient,
        grad_gate_w[None],
        grad_up_w[None],
        grad_down_w[None],
    )


def solution(mesh):
    in_specs = (
        P("expert", None),
        P("expert", None),
        P("expert", None),
        P("expert", None),
        P("expert", None),
        P("expert", None),
        P("expert", None, "tensor"),
        P("expert", None, "tensor"),
        P("expert", "tensor", None),
    )
    out_specs = (
        P("expert", "tensor"),
        P("expert", "tensor"),
        P("expert", None),
        P("expert", None, "tensor"),
        P("expert", None, "tensor"),
        P("expert", "tensor", None),
    )
    return jax.shard_map(local, mesh=mesh, in_specs=in_specs, out_specs=out_specs, check_vma=False)
```

profile of v0, /device:TPU:6, one launch (start us, length us, event | category | flops | bytes accessed | tf_op | source)
XLA Modules:
  0.0 246.5 jit_solution(5502937178036064327)
XLA Ops:
  7.2 0.9 select_reduce_fusion.1
  8.1 0.7 broadcast_compare_fusion
  8.9 0.7 convert_reduce_fusion
  9.6 2.3 fusion.14
  11.8 12.2 %all-to-all-start = ((bf16[64,8,896]{2,1,0:T(8,128)(2,1)}), bf16[64,8,896]{2,1,0:T(8,128)(2,1)S(1)}, u32[]{:S(2)}, u32[]{:S(2)}) async-start(bf16[64,8,896]{2,1,0:T(8,128)(2,1)} %fusion.14), calls=%async_computation | async-start | bytes 1835008 | tf_op jit(solution)/shard_map/all_to_all | solution.py:123
  24.1 1.0 select_reduce_fusion
  25.1 4.2 %multiply_convert_fusion = bf16[512,3584]{1,0:T(8,128)(2,1)} fusion(bf16[128,3584]{1,0:T(8,128)(2,1)} %param.10, f32[512]{0:T(512)S(1)} %select_reduce_fusion, s32[512,128]{1,0:T(8,128)S(1)} %convert_reduce_fusion), kind=kOutput, calls=%fused_computation.2 | convolution fusion | flops 473497600 | bytes 4851712 | tf_op jit(solution)/shard_map/dot_general | solution.py:25
  29.3 18.9 %all-to-all-done = bf16[64,8,896]{2,1,0:T(8,128)(2,1)S(1)} async-done(((bf16[64,8,896]{2,1,0:T(8,128)(2,1)}), bf16[64,8,896]{2,1,0:T(8,128)(2,1)S(1)}, u32[]{:S(2)}, u32[]{:S(2)}) %all-to-all-start) | async-done | bytes 917536 | tf_op jit(solution)/shard_map/all_to_all | solution.py:123
  48.2 0.9 copy-done.2
  49.1 7.9 %all-to-all-start.2 = ((bf16[64,8,3584]{2,1,0:T(8,128)(2,1)}), bf16[64,8,3584]{2,1,0:T(8,128)(2,1)}, u32[]{:S(2)}, u32[]{:S(2)}) async-start(bf16[64,8,3584]{2,1,0:T(8,128)(2,1)} %bitcast.73), calls=%async_computation.3 | async-start | bytes 7340032 | tf_op jit(solution)/shard_map/all_to_all | solution.py:132
  57.1 4.3 %reshape_squeeze.9 = bf16[256,4,896]{2,1,0:T(4,128)(2,1)} reshape(bf16[1,256,3584]{2,1,0:T(8,128)(2,1)} %param.17) | data formatting | bytes 3670016 | tf_op jit(solution)/shard_map/reshape;squeeze | solution.py:67
  61.4 32.8 %all-gather.2.cloned.1.call-done = bf16[512,3584]{1,0:T(8,128)(2,1)} async-done(((bf16[512,896]{1,0:T(8,128)(2,1)}), bf16[512,3584]{1,0:T(8,128)(2,1)}) %all-gather.2.cloned.1.call-update) | async-done | bytes 3670032 | tf_op jit(solution)/shard_map/all_gather | solution.py:131
  94.2 3.9 %fusion.11 = f32[512,256]{1,0:T(8,128)S(1)} fusion(bf16[512,3584]{1,0:T(8,128)(2,1)} %all-gather.2.cloned.1.call-done, bf16[1,3584,256]{2,1,0:T(8,128)(2,1)} %param.15), kind=kOutput, calls=%fused_computation.24 | convolution fusion | flops 939524096 | bytes 6029312 | tf_op jit(solution)/shard_map/dot_general | solution.py:57
  98.1 2.0 multiply_convert_fusion.3
  100.8 3.0 %convert_bitcast_fusion = bf16[4,512,896]{2,1,0:T(8,128)(2,1)} fusion(bf16[256,4,896]{2,1,0:T(4,128)(2,1)S(1)} %copy-done.1, bf16[512,256]{1,0:T(8,128)(2,1)S(1)} %get-tuple-element.14), kind=kOutput, calls=%fused_computation.16 | convolution fusion | flops 941359104 | bytes 5767168 | tf_op jit(solution)/shard_map/mh,hkd->kmd/dot_general | solution.py:68
  104.0 35.7 %all-to-all-done.2 = bf16[64,8,3584]{2,1,0:T(8,128)(2,1)} async-done(((bf16[64,8,3584]{2,1,0:T(8,128)(2,1)}), bf16[64,8,3584]{2,1,0:T(8,128)(2,1)}, u32[]{:S(2)}, u32[]{:S(2)}) %all-to-all-start.2) | async-done | bytes 3670048 | tf_op jit(solution)/shard_map/all_to_all | solution.py:132
  139.7 4.2 %multiply_convert_fusion.1 = (bf16[512,256]{1,0:T(8,128)(2,1)S(1)}, bf16[512,256]{1,0:T(8,128)(2,1)S(1)}) fusion(f32[512,256]{1,0:T(8,128)S(1)} %get-tuple-element.19, f32[512,256]{1,0:T(8,128)S(1)} %fusion.11, f32[512,256]{1,0:T(8,128)} %get-tuple-element.17, f32[512,256]{1,0:T(8,128)} %get-tuple-element.16, bf16[1,256,3584]{2,1,0:T(8,128)(2,1)} %param.17, ...), kind=kOutput, calls=%fused_computation.31 | convolution fusion | flops 940703744 | bytes 8126464 | tf_op jit(solution)/shard_map/dot_general | solution.py:71
  143.9 1.1 fusion.17
  145.0 3.1 %fusion.3 = bf16[4,512,896]{2,1,0:T(8,128)(2,1)} fusion(f32[512,4,896]{2,0,1:T(8,128)S(1)} %fusion.17, bf16[4,896,256]{2,1,0:T(8,128)(2,1)S(1)} %bitcast.71, bf16[512,256]{1,0:T(8,128)(2,1)S(1)} %get-tuple-element.29), kind=kOutput, calls=%fused_computation.9 | convolution fusion | flops 943194112 | bytes 13107200 | tf_op jit(solution)/shard_map/mh,kdh->kmd/dot_general | solution.py:80
  148.2 1.3 reduce-scatter.3.cloned.1.call-done
  149.5 10.7 %all-to-all-start.1 = ((bf16[64,8,896]{2,1,0:T(8,128)(2,1)}), bf16[64,8,896]{2,1,0:T(8,128)(2,1)S(1)}, u32[]{:S(2)}, u32[]{:S(2)}) async-start(bf16[64,8,896]{2,1,0:T(8,128)(2,1)} %bitcast.77), calls=%async_computation.2 | async-start | bytes 1835008 | tf_op jit(solution)/shard_map/all_to_all | solution.py:142
  160.7 1.0 dynamic-slice_convert_fusion
  161.7 35.3 %reduce-scatter.5.cloned.1.call-done = bf16[1,512,896]{2,1,0:T(8,128)(2,1)} async-done(((bf16[4,512,896]{2,1,0:T(8,128)(2,1)}), bf16[1,512,896]{2,1,0:T(8,128)(2,1)}) %reduce-scatter.5.cloned.1.call-update) | async-done | bytes 917520 | tf_op jit(solution)/shard_map/reduce_scatter | solution.py:149
  197.0 10.9 %all-to-all-start.3 = ((bf16[64,8,896]{2,1,0:T(8,128)(2,1)}), bf16[64,8,896]{2,1,0:T(8,128)(2,1)}, u32[]{:S(2)}, u32[]{:S(2)}) async-start(bf16[64,8,896]{2,1,0:T(8,128)(2,1)} %bitcast.76), calls=%async_computation.5 | async-start | bytes 1835008 | tf_op jit(solution)/shard_map/all_to_all | solution.py:150
  207.9 4.6 %fusion.2 = bf16[1,256,3584]{2,1,0:T(8,128)(2,1)} fusion(bf16[512,256]{1,0:T(8,128)(2,1)} %copy-done.4, bf16[64,8,3584]{2,1,0:T(8,128)(2,1)} %all-to-all-done.2), kind=kOutput, calls=%fused_computation.8 | convolution fusion | flops 940441600 | bytes 5767168 | tf_op jit(solution)/shard_map/dot_general | solution.py:88
  212.5 2.4 fusion.1
  214.9 2.4 fusion
  217.3 5.3 %gather_fusion = bf16[1024,896]{1,0:T(8,128)(2,1)} fusion(bf16[512,896]{1,0:T(8,128)(2,1)S(1)} %bitcast.72, s32[1024]{0:T(1024)S(1)} %broadcast_clamp_fusion), kind=kCustom, calls=%fused_computation | custom fusion | bytes 3674112 | tf_op jit(solution)/shard_map/jit(_take)/gather | solution.py:159
  222.6 2.2 fusion.4
  225.1 9.2 %psum.7 = f32[128,8]{0,1:T(8,128)} all-reduce(f32[128,8]{0,1:T(8,128)S(1)} %get-tuple-element.34), channel_id=1, replica_groups=mesh['expert'=64,'tensor'=4] {'tensor'}, use_global_device_ids=true, to_apply=%region_7.8 | all-reduce | flops 1024 | bytes 8192 | tf_op jit(solution)/shard_map/psum | solution.py:174
  234.3 3.5 %multiply_reduce_fusion = bf16[128,896]{1,0:T(8,128)(2,1)} fusion(bf16[1024,896]{1,0:T(8,128)(2,1)} %gather_fusion, f32[128,8]{1,0:T(8,128)S(1)} %copy.33, pred[128,8]{1,0:T(8,128)(4,1)S(1)} %copy.34), kind=kLoop, calls=%fused_computation.15 | loop fusion | flops 3555328 | bytes 2069504 | tf_op jit(solution)/shard_map/reduce_sum | solution.py:164
  237.8 2.2 convolution_convert_fusion.4
  (42 shorter events, 1.6 us)
Async XLA Ops:
  7.2 90.9 %copy-start = (bf16[1,3584,256]{2,1,0:T(8,128)(2,1)S(1)}, bf16[1,3584,256]{2,1,0:T(8,128)(2,1)}, u32[]{:S(2)}) copy-start(bf16[1,3584,256]{2,1,0:T(8,128)(2,1)} %param.16) | copy-start | bytes 5505028
  7.2 16.9 %copy-start.9 = (f32[128,8]{0,1:T(8,128)S(1)}, f32[128,8]{0,1:T(8,128)}, u32[]{:S(2)}) copy-start(f32[128,8]{0,1:T(8,128)} %param.13) | copy-start | bytes 12292
  11.8 36.3 %all-to-all-start = ((bf16[64,8,896]{2,1,0:T(8,128)(2,1)}), bf16[64,8,896]{2,1,0:T(8,128)(2,1)S(1)}, u32[]{:S(2)}, u32[]{:S(2)}) async-start(bf16[64,8,896]{2,1,0:T(8,128)(2,1)} %fusion.14), calls=%async_computation | async-start | bytes 1835008 | tf_op jit(solution)/shard_map/all_to_all | solution.py:123
  24.0 70.2 %all-gather.2.cloned.1.call-start = ((), (), s32[]{:S(2)}) async-start(), calls=%async_computation.6 | async-start | bytes 4587520 | tf_op jit(solution)/shard_map/all_gather | solution.py:131
  48.2 0.9 copy-start.2
  49.1 90.5 %all-to-all-start.2 = ((bf16[64,8,3584]{2,1,0:T(8,128)(2,1)}), bf16[64,8,3584]{2,1,0:T(8,128)(2,1)}, u32[]{:S(2)}, u32[]{:S(2)}) async-start(bf16[64,8,3584]{2,1,0:T(8,128)(2,1)} %bitcast.73), calls=%async_computation.3 | async-start | bytes 7340032 | tf_op jit(solution)/shard_map/all_to_all | solution.py:132
  57.1 92.4 %reduce-scatter.3.cloned.1.call-start = ((), (), s32[]{:S(2)}) async-start(), calls=%async_computation.7 | async-start | bytes 4587520 | tf_op jit(solution)/shard_map/reduce_scatter | solution.py:140
  94.2 3.9 %copy-start.10 = (bf16[512,3584]{1,0:T(8,128)(2,1)S(1)}, bf16[512,3584]{1,0:T(8,128)(2,1)}, u32[]{:S(2)}) copy-start(bf16[512,3584]{1,0:T(8,128)(2,1)} %all-gather.2.cloned.1.call-done) | copy-start | bytes 11010052
  98.1 2.7 %copy-start.1 = (bf16[256,4,896]{2,1,0:T(4,128)(2,1)S(1)}, bf16[256,4,896]{2,1,0:T(4,128)(2,1)}, u32[]{:S(2)}) copy-start(bf16[256,4,896]{2,1,0:T(4,128)(2,1)} %reshape_squeeze.9) | copy-start | bytes 5505028
  100.1 0.7 copy-start.4
  103.9 93.0 %reduce-scatter.5.cloned.1.call-start = ((), (), s32[]{:S(2)}) async-start(), calls=%async_computation.8 | async-start | bytes 4587520 | tf_op jit(solution)/shard_map/reduce_scatter | solution.py:149
  139.7 4.2 %copy-start.3 = (bf16[1,3584,256]{2,1,0:T(8,128)(2,1)S(1)}, bf16[1,3584,256]{2,1,0:T(8,128)(2,1)}, u32[]{:S(2)}) copy-start(bf16[1,3584,256]{2,1,0:T(8,128)(2,1)} %param.15) | copy-start | bytes 5505028
  143.8 1.2 copy-start.5
  143.8 1.2 copy-start.7
  149.5 47.5 %all-to-all-start.1 = ((bf16[64,8,896]{2,1,0:T(8,128)(2,1)}), bf16[64,8,896]{2,1,0:T(8,128)(2,1)S(1)}, u32[]{:S(2)}, u32[]{:S(2)}) async-start(bf16[64,8,896]{2,1,0:T(8,128)(2,1)} %bitcast.77), calls=%async_computation.2 | async-start | bytes 1835008 | tf_op jit(solution)/shard_map/all_to_all | solution.py:142
  197.0 40.8 %all-to-all-start.3 = ((bf16[64,8,896]{2,1,0:T(8,128)(2,1)}), bf16[64,8,896]{2,1,0:T(8,128)(2,1)}, u32[]{:S(2)}, u32[]{:S(2)}) async-start(bf16[64,8,896]{2,1,0:T(8,128)(2,1)} %bitcast.76), calls=%async_computation.5 | async-start | bytes 1835008 | tf_op jit(solution)/shard_map/all_to_all | solution.py:150
  207.9 4.7 %copy-start.8 = (bf16[512,256]{1,0:T(8,128)(2,1)S(1)}, bf16[512,256]{1,0:T(8,128)(2,1)}, u32[]{:S(2)}) copy-start(bf16[512,256]{1,0:T(8,128)(2,1)} %copy-done.7) | copy-start | bytes 786436
  207.9 4.7 %copy-start.11 = (bf16[512,3584]{1,0:T(8,128)(2,1)S(1)}, bf16[512,3584]{1,0:T(8,128)(2,1)}, u32[]{:S(2)}) copy-start(bf16[512,3584]{1,0:T(8,128)(2,1)} %all-gather.2.cloned.1.call-done) | copy-start | bytes 11010052
  212.5 2.4 copy-start.6
Sparse Core Ops, SparseCore 0:
  49.3 44.9 all-gather.1
  104.0 45.4 reduce-scatter.2
  152.0 44.8 reduce-scatter.4
where the time goes:
time: 247 us
  waiting for transfers between devices  124 us (50%)
  starting transfers between devices  41.9 us (17%)
  matrix products  35.5 us (14%)
  between operations  14 us (6%)
  local copies, waits for them, and re-layouts  11.9 us (5%)
  other arithmetic  10.2 us (4%)
  blocking collectives  9.16 us (4%)
    all_to_all x1, waiting for transfers between devices, local(): lax.all_to_all(cot_rows.reshape(expert_number, expert_capacity, feature_w...  35.7 us
    reduce_scatter x1, waiting for transfers between devices, local(): lax.psum_scatter(back_t, 'tensor', scatter_dimension=0, tiled=True)  35.3 us
    all_gather x1, waiting for transfers between devices, local(): rows_all = lax.all_gather(rows_q, 'tensor', axis=1, tiled=True)  32.8 us
    all_to_all x1, waiting for transfers between devices, local(): lax.all_to_all(token_sum.reshape(expert_number, expert_capacity, feature_...  18.9 us
    all_to_all x1, starting transfers between devices, local(): lax.all_to_all(token_sum.reshape(expert_number, expert_capacity, feature_...  12.2 us
    all_to_all x1, starting transfers between devices, local(): lax.all_to_all(total_back.reshape(sources, expert_capacity, feature_share...  10.9 us
    all_to_all x1, starting transfers between devices, local(): lax.all_to_all(total_out.reshape(sources, expert_capacity, feature_share)...  10.7 us
    psum x1, blocking collectives, local(): lax.psum(jnp.where(slot_alive_mask, hidden_totals, 0.0), 'tensor')  9.16 us
  transfers between devices with their start and end apart: 7, of which 5 were waited for; matrix products, arithmetic and copies ran while one was open for 20% of the time, Pallas kernels for 0%

commit v1 on v0

--- a/solution.py
+++ b/solution.py
@@ -128,7 +128,23 @@
         tiled=True,
     ).reshape(send_rows, feature_share)
     rows_q, cot_rows = lax.optimization_barrier((rows_q, cot_rows))
-    rows_all = lax.all_gather(rows_q, "tensor", axis=1, tiled=True)
+    ways, here, step = (lax.axis_size("tensor"), lax.axis_index("tensor"), rows_q.shape[1])
+    lengths = [n * ways if d == 1 else n for d, n in enumerate(rows_q.shape)]
+    full = lax.dynamic_update_slice_in_dim(
+        jnp.zeros(lengths, rows_q.dtype), rows_q, here * step, axis=1
+    )
+    going_up = going_down = rows_q
+    for far in range(1, ways // 2 + 1):
+        going_up = lax.ppermute(going_up, "tensor", [(d, (d + 1) % ways) for d in range(ways)])
+        full = lax.dynamic_update_slice_in_dim(full, going_up, (here - far) % ways * step, axis=1)
+        if 2 * far < ways:
+            going_down = lax.ppermute(
+                going_down, "tensor", [(d, (d - 1) % ways) for d in range(ways)]
+            )
+            full = lax.dynamic_update_slice_in_dim(
+                full, going_down, (here + far) % ways * step, axis=1
+            )
+    rows_all = full
     cots_all = lax.all_to_all(
         cot_rows.reshape(expert_number, expert_capacity, feature_width),
         "expert",

time: 247 us -> 270 us (1.093)
  waiting for transfers between devices: 124 us -> 144 us
  local copies, waits for them, and re-layouts: 11.9 us -> 15.3 us
  matrix products: 35.5 us -> 32.4 us
    all_gather x1 -> x0, waiting for transfers between devices: 32.8 us -> none  [local(): rows_all = lax.all_gather(rows_q, 'tensor', axis=1, tiled=True)]
    ppermute x0 -> x3, waiting for transfers between devices: none -> 29.6 us  [the longest x2 29.6 us: local(): lax.ppermute(going_up, 'tensor', [(d, (d + 1) % ways) for d in range(ways)])]
    all_to_all x1, waiting for transfers between devices: 35.7 us -> 62 us  [local(): lax.all_to_all(cot_rows.reshape(expert_number, expert_capacity, feature_w...]
    reduce_scatter x1, waiting for transfers between devices: 35.3 us -> 11.6 us  [local(): lax.psum_scatter(back_t, 'tensor', scatter_dimension=0, tiled=True)]
    all_to_all x1, waiting for transfers between devices: 0.01 us -> 22.7 us  [local(): lax.all_to_all(total_out.reshape(sources, expert_capacity, feature_share)...]
    dynamic_update_slice x0 -> x4, local copies, waits for them, and re-layouts: none -> 4.18 us  [the longest x2 2.73 us: local(): lax.dynamic_update_slice_in_dim(full, going_up, (here - far) % ways * ste...]
    ppermute x0 -> x3, starting transfers between devices: none -> 3.67 us  [the longest x2 2.01 us: local(): lax.ppermute(going_up, 'tensor', [(d, (d + 1) % ways) for d in range(ways)])]
    all_to_all x1, starting transfers between devices: 10.7 us -> 7.8 us  [local(): lax.all_to_all(total_out.reshape(sources, expert_capacity, feature_share)...]
  transfers between devices with their start and end apart: 7 -> 9, of which waited for: 5 -> 6; matrix products, arithmetic and copies ran while one was open for 20% -> 19% of each run, Pallas kernels for 0% -> 0%
where the time goes in v1:
time: 270 us; the launch traced here: 269 us
  waiting for transfers between devices  144 us (53%)
  starting transfers between devices  42.3 us (16%)
  matrix products  32.4 us (12%)
  local copies, waits for them, and re-layouts  15.3 us (6%)
  between operations  14.3 us (5%)
  other arithmetic  11.1 us (4%)
  blocking collectives  9.17 us (3%)
    all_to_all x1, waiting for transfers between devices, local(): lax.all_to_all(cot_rows.reshape(expert_number, expert_capacity, feature_w...  62 us
    ppermute x2, waiting for transfers between devices, local(): lax.ppermute(going_up, 'tensor', [(d, (d + 1) % ways) for d in range(ways)])  29.6 us
    all_to_all x1, waiting for transfers between devices, local(): lax.all_to_all(total_out.reshape(sources, expert_capacity, feature_share)...  22.7 us
    all_to_all x1, waiting for transfers between devices, local(): lax.all_to_all(token_sum.reshape(expert_number, expert_capacity, feature_...  18.2 us
    all_to_all x1, starting transfers between devices, local(): lax.all_to_all(token_sum.reshape(expert_number, expert_capacity, feature_...  12.2 us
    reduce_scatter x1, waiting for transfers between devices, local(): lax.psum_scatter(back_t, 'tensor', scatter_dimension=0, tiled=True)  11.6 us
    all_to_all x1, starting transfers between devices, local(): lax.all_to_all(total_back.reshape(sources, expert_capacity, feature_share...  10.9 us
    psum x1, blocking collectives, local(): lax.psum(jnp.where(slot_alive_mask, hidden_totals, 0.0), 'tensor')  9.17 us
  transfers between devices with their start and end apart: 9, of which 6 were waited for; matrix products, arithmetic and copies ran while one was open for 19% of the time, Pallas kernels for 0%

profile of v1, /device:TPU:6, one launch (start us, length us, event | category | flops | bytes accessed | tf_op | source)
XLA Modules:
  0.0 268.8 jit_solution(9174965412390799929)
XLA Ops:
  9.6 2.3 fusion.14
  11.8 12.2 %all-to-all-start = ((bf16[64,8,896]{2,1,0:T(8,128)(2,1)}), bf16[64,8,896]{2,1,0:T(8,128)(2,1)S(1)}, u32[]{:S(2)}, u32[]{:S(2)}) async-start(bf16[64,8,896]{2,1,0:T(8,128)(2,1)} %fusion.14), calls=%async_computation | async-start | bytes 1835008 | tf_op jit(solution)/shard_map/all_to_all | solution.py:123
  24.0 1.7 select_reduce_fusion
  25.7 4.2 %multiply_convert_fusion = bf16[512,3584]{1,0:T(8,128)(2,1)} fusion(bf16[128,3584]{1,0:T(8,128)(2,1)} %param.10, f32[512]{0:T(512)S(1)} %select_reduce_fusion, s32[512,128]{1,0:T(8,128)S(1)} %convert_reduce_fusion), kind=kOutput, calls=%fused_computation.2 | convolution fusion | flops 473497600 | bytes 4851712 | tf_op jit(solution)/shard_map/dot_general | solution.py:25
  29.9 18.2 %all-to-all-done = bf16[64,8,896]{2,1,0:T(8,128)(2,1)S(1)} async-done(((bf16[64,8,896]{2,1,0:T(8,128)(2,1)}), bf16[64,8,896]{2,1,0:T(8,128)(2,1)S(1)}, u32[]{:S(2)}, u32[]{:S(2)}) %all-to-all-start) | async-done | bytes 917536 | tf_op jit(solution)/shard_map/all_to_all | solution.py:123
  48.2 1.6 collective-permute-start
  49.7 1.7 collective-permute-start.1
  51.4 20.7 %collective-permute-done = bf16[512,896]{1,0:T(8,128)(2,1)} collective-permute-done((bf16[512,896]{1,0:T(8,128)(2,1)S(1)}, bf16[512,896]{1,0:T(8,128)(2,1)}, u32[]{:S(2)}, u32[]{:S(2)}) %collective-permute-start) | collective-permute-done | bytes 917536 | tf_op jit(solution)/shard_map/ppermute | solution.py:138
  72.5 4.2 %reshape_squeeze.9 = bf16[256,4,896]{2,1,0:T(4,128)(2,1)} reshape(bf16[1,256,3584]{2,1,0:T(8,128)(2,1)} %param.17) | data formatting | bytes 3670016 | tf_op jit(solution)/shard_map/reshape;squeeze | solution.py:67
  76.7 7.5 %all-to-all-start.2 = ((bf16[64,8,3584]{2,1,0:T(8,128)(2,1)}), bf16[64,8,3584]{2,1,0:T(8,128)(2,1)}, u32[]{:S(2)}, u32[]{:S(2)}) async-start(bf16[64,8,3584]{2,1,0:T(8,128)(2,1)} %bitcast.69), calls=%async_computation.3 | async-start | bytes 7340032 | tf_op jit(solution)/shard_map/all_to_all | solution.py:148
  84.6 1.4 constant_dynamic-update-slice_fusion.2
  86.1 1.3 constant_dynamic-update-slice_fusion.1
  87.4 8.9 %collective-permute-done.2 = bf16[512,896]{1,0:T(8,128)(2,1)} collective-permute-done((bf16[512,896]{1,0:T(8,128)(2,1)}, bf16[512,896]{1,0:T(8,128)(2,1)}, u32[]{:S(2)}, u32[]{:S(2)}) %collective-permute-start.2) | collective-permute-done | bytes 917536 | tf_op jit(solution)/shard_map/ppermute | solution.py:138
  96.3 1.3 constant_dynamic-update-slice_fusion
  98.8 2.0 multiply_convert_fusion.3
  101.5 3.0 %convert_bitcast_fusion = bf16[4,512,896]{2,1,0:T(8,128)(2,1)} fusion(bf16[256,4,896]{2,1,0:T(4,128)(2,1)S(1)} %copy-done.1, bf16[512,256]{1,0:T(8,128)(2,1)S(1)} %get-tuple-element.14), kind=kOutput, calls=%fused_computation.16 | convolution fusion | flops 941359104 | bytes 5767168 | tf_op jit(solution)/shard_map/mh,hkd->kmd/dot_general | solution.py:68
  104.8 62.0 %all-to-all-done.2 = bf16[64,8,3584]{2,1,0:T(8,128)(2,1)} async-done(((bf16[64,8,3584]{2,1,0:T(8,128)(2,1)}), bf16[64,8,3584]{2,1,0:T(8,128)(2,1)}, u32[]{:S(2)}, u32[]{:S(2)}) %all-to-all-start.2) | async-done | bytes 3670048 | tf_op jit(solution)/shard_map/all_to_all | solution.py:148
  166.8 3.9 %fusion.6 = f32[512,256]{1,0:T(8,128)S(1)} fusion(bf16[64,8,3584]{2,1,0:T(8,128)(2,1)} %all-to-all-done.2, bf16[1,256,3584]{2,1,0:T(8,128)(2,1)} %param.17), kind=kOutput, calls=%fused_computation.13 | convolution fusion | flops 939524096 | bytes 6029312 | tf_op jit(solution)/shard_map/dot_general | solution.py:71
  171.0 1.2 fusion.17
  172.2 3.1 %fusion.3 = bf16[4,512,896]{2,1,0:T(8,128)(2,1)} fusion(f32[512,4,896]{2,0,1:T(8,128)S(1)} %fusion.17, bf16[4,896,256]{2,1,0:T(8,128)(2,1)S(1)} %bitcast.67, bf16[512,256]{1,0:T(8,128)(2,1)S(1)} %get-tuple-element.29), kind=kOutput, calls=%fused_computation.9 | convolution fusion | flops 943194112 | bytes 13107200 | tf_op jit(solution)/shard_map/mh,kdh->kmd/dot_general | solution.py:80
  175.4 7.8 %all-to-all-start.1 = ((bf16[64,8,896]{2,1,0:T(8,128)(2,1)}), bf16[64,8,896]{2,1,0:T(8,128)(2,1)S(1)}, u32[]{:S(2)}, u32[]{:S(2)}) async-start(bf16[64,8,896]{2,1,0:T(8,128)(2,1)} %bitcast.75), calls=%async_computation.2 | async-start | bytes 1835008 | tf_op jit(solution)/shard_map/all_to_all | solution.py:158
  184.6 22.7 %all-to-all-done.1 = bf16[64,8,896]{2,1,0:T(8,128)(2,1)S(1)} async-done(((bf16[64,8,896]{2,1,0:T(8,128)(2,1)}), bf16[64,8,896]{2,1,0:T(8,128)(2,1)S(1)}, u32[]{:S(2)}, u32[]{:S(2)}) %all-to-all-start.1) | async-done | bytes 917536 | tf_op jit(solution)/shard_map/all_to_all | solution.py:158
  207.3 11.6 %reduce-scatter.5.cloned.1.call-done = bf16[1,512,896]{2,1,0:T(8,128)(2,1)} async-done(((bf16[4,512,896]{2,1,0:T(8,128)(2,1)}), bf16[1,512,896]{2,1,0:T(8,128)(2,1)}) %reduce-scatter.5.cloned.1.call-update) | async-done | bytes 917520 | tf_op jit(solution)/shard_map/reduce_scatter | solution.py:165
  218.9 10.9 %all-to-all-start.3 = ((bf16[64,8,896]{2,1,0:T(8,128)(2,1)}), bf16[64,8,896]{2,1,0:T(8,128)(2,1)}, u32[]{:S(2)}, u32[]{:S(2)}) async-start(bf16[64,8,896]{2,1,0:T(8,128)(2,1)} %bitcast.74), calls=%async_computation.5 | async-start | bytes 1835008 | tf_op jit(solution)/shard_map/all_to_all | solution.py:166
  229.8 4.6 %fusion.2 = bf16[1,256,3584]{2,1,0:T(8,128)(2,1)} fusion(bf16[512,256]{1,0:T(8,128)(2,1)} %copy-done.6, bf16[64,8,3584]{2,1,0:T(8,128)(2,1)} %all-to-all-done.2), kind=kOutput, calls=%fused_computation.8 | convolution fusion | flops 940441600 | bytes 5767168 | tf_op jit(solution)/shard_map/dot_general | solution.py:88
  234.5 2.4 fusion.1
  236.9 2.4 fusion
  239.3 5.3 %gather_fusion = bf16[1024,896]{1,0:T(8,128)(2,1)} fusion(bf16[512,896]{1,0:T(8,128)(2,1)S(1)} %bitcast.68, s32[1024]{0:T(1024)S(1)} %broadcast_clamp_fusion), kind=kCustom, calls=%fused_computation | custom fusion | bytes 3674112 | tf_op jit(solution)/shard_map/jit(_take)/gather | solution.py:175
  244.6 2.2 fusion.4
  247.1 9.2 %psum.7 = f32[128,8]{0,1:T(8,128)} all-reduce(f32[128,8]{0,1:T(8,128)S(1)} %get-tuple-element.34), channel_id=1, replica_groups=mesh['expert'=64,'tensor'=4] {'tensor'}, use_global_device_ids=true, to_apply=%region_7.8 | all-reduce | flops 1024 | bytes 8192 | tf_op jit(solution)/shard_map/psum | solution.py:190
  256.3 3.5 %multiply_reduce_fusion = bf16[128,896]{1,0:T(8,128)(2,1)} fusion(bf16[1024,896]{1,0:T(8,128)(2,1)} %gather_fusion, f32[128,8]{1,0:T(8,128)S(1)} %copy.33, pred[128,8]{1,0:T(8,128)(4,1)S(1)} %copy.34), kind=kLoop, calls=%fused_computation.15 | loop fusion | flops 3555328 | bytes 2069504 | tf_op jit(solution)/shard_map/reduce_sum | solution.py:180
  259.8 2.2 convolution_convert_fusion.4
  (55 shorter events, 7.3 us)
Async XLA Ops:
  7.2 91.6 %copy-start = (bf16[1,3584,256]{2,1,0:T(8,128)(2,1)S(1)}, bf16[1,3584,256]{2,1,0:T(8,128)(2,1)}, u32[]{:S(2)}) copy-start(bf16[1,3584,256]{2,1,0:T(8,128)(2,1)} %param.16) | copy-start | bytes 5505028
  11.8 36.3 %all-to-all-start = ((bf16[64,8,896]{2,1,0:T(8,128)(2,1)}), bf16[64,8,896]{2,1,0:T(8,128)(2,1)S(1)}, u32[]{:S(2)}, u32[]{:S(2)}) async-start(bf16[64,8,896]{2,1,0:T(8,128)(2,1)} %fusion.14), calls=%async_computation | async-start | bytes 1835008 | tf_op jit(solution)/shard_map/all_to_all | solution.py:123
  48.2 23.9 %collective-permute-start = (bf16[512,896]{1,0:T(8,128)(2,1)S(1)}, bf16[512,896]{1,0:T(8,128)(2,1)}, u32[]{:S(2)}, u32[]{:S(2)}) collective-permute-start(bf16[512,896]{1,0:T(8,128)(2,1)S(1)} %bitcast.70), channel_id=1, source_target_pairs={{0,1},{1,2},{2,3},{3,0},{4,5},{5,6},{6,7},{7,4},{8,9},{9,10},{10,1... | collective-permute-start | bytes 2752520 | tf_op jit(solution)/shard_map/ppermute | solution.py:138
  49.7 36.3 %collective-permute-start.1 = (bf16[512,896]{1,0:T(8,128)(2,1)S(1)}, bf16[512,896]{1,0:T(8,128)(2,1)}, u32[]{:S(2)}, u32[]{:S(2)}) collective-permute-start(bf16[512,896]{1,0:T(8,128)(2,1)S(1)} %bitcast.71), channel_id=1, source_target_pairs={{0,3},{1,0},{2,1},{3,2},{4,7},{5,4},{6,5},{7,6},{8,11},{9,8},{10,9... | collective-permute-start | bytes 2752520 | tf_op jit(solution)/shard_map/ppermute | solution.py:141
  72.1 24.3 %collective-permute-start.2 = (bf16[512,896]{1,0:T(8,128)(2,1)}, bf16[512,896]{1,0:T(8,128)(2,1)}, u32[]{:S(2)}, u32[]{:S(2)}) collective-permute-start(bf16[512,896]{1,0:T(8,128)(2,1)} %collective-permute-done), channel_id=1, source_target_pairs={{0,1},{1,2},{2,3},{3,0},{4,5},{5,6},{6,7},{7,4},{8,9},{9,10},{10,1... | collective-permute-start | bytes 2752520 | tf_op jit(solution)/shard_map/ppermute | solution.py:138
  76.7 90.1 %all-to-all-start.2 = ((bf16[64,8,3584]{2,1,0:T(8,128)(2,1)}), bf16[64,8,3584]{2,1,0:T(8,128)(2,1)}, u32[]{:S(2)}, u32[]{:S(2)}) async-start(bf16[64,8,3584]{2,1,0:T(8,128)(2,1)} %bitcast.69), calls=%async_computation.3 | async-start | bytes 7340032 | tf_op jit(solution)/shard_map/all_to_all | solution.py:148
  84.2 91.2 %reduce-scatter.3.cloned.1.call-start = ((), (), s32[]{:S(2)}) async-start(), calls=%async_computation.6 | async-start | bytes 4587520 | tf_op jit(solution)/shard_map/reduce_scatter | solution.py:156
  84.5 13.1 %copy-start.4 = (bf16[1,3584,256]{2,1,0:T(8,128)(2,1)S(1)}, bf16[1,3584,256]{2,1,0:T(8,128)(2,1)}, u32[]{:S(2)}) copy-start(bf16[1,3584,256]{2,1,0:T(8,128)(2,1)} %param.15) | copy-start | bytes 5505028
  97.6 3.2 %copy-start.2 = (bf16[512,3584]{1,0:T(8,128)(2,1)}, bf16[512,3584]{1,0:T(8,128)(2,1)S(1)}, u32[]{:S(2)}) copy-start(bf16[512,3584]{1,0:T(8,128)(2,1)S(1)} %constant_dynamic-update-slice_fusion) | copy-start | bytes 11010052
  98.8 2.7 %copy-start.1 = (bf16[256,4,896]{2,1,0:T(4,128)(2,1)S(1)}, bf16[256,4,896]{2,1,0:T(4,128)(2,1)}, u32[]{:S(2)}) copy-start(bf16[256,4,896]{2,1,0:T(4,128)(2,1)} %reshape_squeeze.9) | copy-start | bytes 5505028
  100.8 0.7 copy-start.6
  104.6 114.4 %reduce-scatter.5.cloned.1.call-start = ((), (), s32[]{:S(2)}) async-start(), calls=%async_computation.7 | async-start | bytes 4587520 | tf_op jit(solution)/shard_map/reduce_scatter | solution.py:165
  166.8 3.9 %copy-start.11 = (f32[512,256]{1,0:T(8,128)S(1)}, f32[512,256]{1,0:T(8,128)}, u32[]{:S(2)}) copy-start(f32[512,256]{1,0:T(8,128)} %get-tuple-element.17) | copy-start | bytes 1572868
  166.8 3.9 %copy-start.12 = (f32[512,256]{1,0:T(8,128)S(1)}, f32[512,256]{1,0:T(8,128)}, u32[]{:S(2)}) copy-start(f32[512,256]{1,0:T(8,128)} %get-tuple-element.16) | copy-start | bytes 1572868
  166.8 4.2 %copy-start.5 = (bf16[1,3584,256]{2,1,0:T(8,128)(2,1)S(1)}, bf16[1,3584,256]{2,1,0:T(8,128)(2,1)}, u32[]{:S(2)}) copy-start(bf16[1,3584,256]{2,1,0:T(8,128)(2,1)} %param.15) | copy-start | bytes 5505028
  171.0 1.2 copy-start.7
  171.0 1.2 copy-start.9
  175.4 32.0 %all-to-all-start.1 = ((bf16[64,8,896]{2,1,0:T(8,128)(2,1)}), bf16[64,8,896]{2,1,0:T(8,128)(2,1)S(1)}, u32[]{:S(2)}, u32[]{:S(2)}) async-start(bf16[64,8,896]{2,1,0:T(8,128)(2,1)} %bitcast.75), calls=%async_computation.2 | async-start | bytes 1835008 | tf_op jit(solution)/shard_map/all_to_all | solution.py:158
  218.9 40.9 %all-to-all-start.3 = ((bf16[64,8,896]{2,1,0:T(8,128)(2,1)}), bf16[64,8,896]{2,1,0:T(8,128)(2,1)}, u32[]{:S(2)}, u32[]{:S(2)}) async-start(bf16[64,8,896]{2,1,0:T(8,128)(2,1)} %bitcast.74), calls=%async_computation.5 | async-start | bytes 1835008 | tf_op jit(solution)/shard_map/all_to_all | solution.py:166
  229.8 4.7 %copy-start.3 = (bf16[512,3584]{1,0:T(8,128)(2,1)S(1)}, bf16[512,3584]{1,0:T(8,128)(2,1)}, u32[]{:S(2)}) copy-start(bf16[512,3584]{1,0:T(8,128)(2,1)} %copy-done.2) | copy-start | bytes 11010052
  229.8 4.7 %copy-start.10 = (bf16[512,256]{1,0:T(8,128)(2,1)S(1)}, bf16[512,256]{1,0:T(8,128)(2,1)}, u32[]{:S(2)}) copy-start(bf16[512,256]{1,0:T(8,128)(2,1)} %copy-done.9) | copy-start | bytes 786436
  234.5 2.4 copy-start.8
  239.3 7.7 %copy-start.13 = (f32[128,8]{0,1:T(8,128)S(1)}, f32[128,8]{0,1:T(8,128)}, u32[]{:S(2)}) copy-start(f32[128,8]{0,1:T(8,128)} %param.13) | copy-start | bytes 12292
Sparse Core Ops, SparseCore 0:
  104.7 40.1 reduce-scatter.2
  175.4 43.4 reduce-scatter.4
